TPU v7x, 32 devices: a whole 2x2x4 slice. The times are simulated.
32 devices in a mesh: wave: 4 (over y, core), lev: 4 (over z), cpl: 2 (over x).
Axes of the slice: x: 2, y: 2, z: 4, core: 2. Of those that a mesh axis runs over, the one named last changes fastest.
Arguments:
- spectral: bfloat16 [1280, 2, 4, 24, 1280], P('wave', None, None, 'lev'), may hold values from -0.125 to 0.125
- legendre: bfloat16 [1280, 16, 1280], P('wave', 'cpl'), may hold values from -0.15625 to 0.15625
- wavenumber: int32 [1280], replicated, may hold values from 0 to 1279, each once
- level_weight: float32 [24], P('lev'), may hold values from 0.1 to 1
- source_row: int32 [16], replicated, may hold values from 0 to 14
- row_weight: float32 [16], replicated, may hold values from 0.2 to 0.8
Outputs:
- ocean_flux: float32 [16, 4, 4320], P(('wave', 'cpl'), None, 'lev')
All inputs are finite; a program needn't handle non-finite values.
Results may differ from a plain program's by a relative error of at most 0.0041.
Values may be sent and summed in bfloat16 or wider, within the bound.
No kernel may reach another device: no remote copies, remote signals or barrier semaphores. Data moves between devices by JAX's collectives and lax.ppermute only.
A program may use at most 192 MiB of HBM per device.

v0:
```python
import math
import jax
import jax.numpy as jnp
from jax import lax
from jax.sharding import PartitionSpec as P

NLON = 4320
LANE = 128


def phase_angle(phase, lon_total):
    return phase.astype(jnp.float32) * (2.0 * math.pi / lon_total)


def surface_flux(grid_vals, level_weight):
    wind_speed = jnp.sqrt(grid_vals[:, 0] ** 2 + grid_vals[:, 1] ** 2 + 0.25)
    return jnp.sum(level_weight[:, None] * wind_speed[:, None] * grid_vals, axis=2)


def latitude_order(gathered, wave_count, cpl_count, lat_dev):
    trailing = gathered.shape[1:]
    gathered = gathered.reshape((wave_count, cpl_count, lat_dev) + trailing)
    gathered = jnp.swapaxes(gathered, 0, 1)
    return gathered.reshape((wave_count * cpl_count * lat_dev,) + trailing)


def interpolate(gathered, source, weight_hi):
    lower = jnp.take(gathered, source, axis=0)
    upper = jnp.take(gathered, source + 1, axis=0)
    return (1.0 - weight_hi[:, None, None]) * lower + weight_hi[:, None, None] * upper


def quarter_tables(wavenumber, width):
    blocks = width // LANE
    factor = jnp.where(wavenumber == 0, 1.0, 2.0).astype(jnp.float32)[:, None]
    offsets = jnp.arange(LANE, dtype=jnp.int32)
    base_angle = phase_angle(wavenumber[:, None] * offsets[None, :] % NLON, NLON)
    base_cos = jnp.cos(base_angle)[:, None, :]
    base_sin = jnp.sin(base_angle)[:, None, :]
    starts = jnp.arange(blocks, dtype=jnp.int32) * LANE
    start_angle = phase_angle(wavenumber[:, None] * starts[None, :] % NLON, NLON)
    start_cos = (factor * jnp.cos(start_angle))[:, :, None]
    start_sin = (factor * jnp.sin(start_angle))[:, :, None]
    cos_tab = start_cos * base_cos - start_sin * base_sin
    sin_tab = start_sin * base_cos + start_cos * base_sin
    slots = wavenumber.shape[0]
    return (
        cos_tab.astype(jnp.bfloat16).reshape(slots, width),
        (-sin_tab).astype(jnp.bfloat16).reshape(slots, width),
    )


def local(spectral, legendre, wavenumber, level_weight, source_row, row_weight):
    slot_count = spectral.shape[0]
    fields = spectral.shape[2]
    levels = spectral.shape[3]
    degree = spectral.shape[4]
    channels = 2 * fields * levels
    wave_count = lax.axis_size("wave")
    cpl_count = lax.axis_size("cpl")
    lev_count = lax.axis_size("lev")
    wave_at = lax.axis_index("wave")
    cpl_at = lax.axis_index("cpl")
    owned_waves = lax.dynamic_slice_in_dim(wavenumber, wave_at * slot_count, slot_count)
    in_triangle = (
        lax.broadcasted_iota(jnp.int32, (slot_count, 1, degree), 2)
        < (degree - owned_waves)[:, None, None]
    )
    table_rows = jnp.where(in_triangle, legendre, jnp.zeros_like(legendre))
    coefficient = spectral.reshape(slot_count, channels, degree)
    spec_grid = jnp.einsum(
        "skj,slj->slk", coefficient, table_rows, preferred_element_type=jnp.float32
    ).astype(jnp.bfloat16)
    by_latitude = lax.all_to_all(spec_grid, "wave", split_axis=1, concat_axis=0, tiled=True)
    total_slots = by_latitude.shape[0]
    lat_dev = by_latitude.shape[1]
    rows = lat_dev * fields * levels
    parts = by_latitude.reshape(total_slots, lat_dev, 2, fields * levels)
    real = parts[:, :, 0].reshape(total_slots, rows).T
    imag = parts[:, :, 1].reshape(total_slots, rows).T
    parity = (1 - 2 * (wavenumber & 1)).astype(jnp.bfloat16)[None, :]
    lhs_cos = jnp.concatenate([real, real * parity], axis=0)
    lhs_sin = jnp.concatenate([imag, imag * parity], axis=0)
    quarter = NLON // 4
    width = -(-(quarter + 1) // LANE) * LANE
    cos_tab, sin_tab = quarter_tables(wavenumber, width)
    r_all = jnp.dot(lhs_cos, cos_tab, preferred_element_type=jnp.float32)
    q_all = jnp.dot(lhs_sin, sin_tab, preferred_element_type=jnp.float32)
    r1, r2 = (r_all[:rows], r_all[rows:])
    q1, q2 = (q_all[:rows], q_all[rows:])

    def flux_of(grid_rows):
        return surface_flux(grid_rows.reshape(lat_dev, fields, levels, quarter), level_weight)

    strip0 = flux_of((r1 + q1)[:, :quarter])
    strip1 = jnp.flip(flux_of((r2 - q2)[:, 1 : quarter + 1]), axis=-1)
    strip2 = flux_of((r2 + q2)[:, :quarter])
    strip3 = jnp.flip(flux_of((r1 - q1)[:, 1 : quarter + 1]), axis=-1)
    partial_value = jnp.concatenate([strip0, strip1, strip2, strip3], axis=-1)
    own_first = (wave_at * cpl_count + cpl_at) * lat_dev
    source = lax.dynamic_slice_in_dim(source_row, own_first, lat_dev)
    weight_hi = lax.dynamic_slice_in_dim(row_weight, own_first, lat_dev)
    strip_width = NLON // lev_count
    by_strip = partial_value.reshape(lat_dev, fields, lev_count, strip_width).transpose(2, 0, 1, 3)
    summed = jnp.sum(
        lax.all_to_all(by_strip, "lev", split_axis=0, concat_axis=0, tiled=True), axis=0
    )
    copies = jnp.broadcast_to(summed[None], (wave_count * cpl_count,) + summed.shape)
    gathered = lax.all_to_all(copies, ("wave", "cpl"), split_axis=0, concat_axis=0, tiled=True)
    gathered = gathered.reshape((wave_count * cpl_count * lat_dev,) + summed.shape[1:])
    gathered = latitude_order(gathered, wave_count, cpl_count, lat_dev)
    return interpolate(gathered, source, weight_hi)


def solution(mesh):
    placed = (P("wave", None, None, "lev", None), P("wave", "cpl", None), P(), P("lev"), P(), P())
    return jax.shard_map(
        local,
        mesh=mesh,
        in_specs=placed,
        out_specs=P(("wave", "cpl"), None, "lev"),
        check_vma=False,
    )
```

profile of v0, /device:TPU:0, one launch (start us, length us, event | category | flops | bytes accessed | tf_op | source)
XLA Modules:
  0.0 121.1 jit_solution(9876910115910982764)
XLA Ops:
  0.0 0.8 dynamic-slice_subtract_fusion
  0.8 0.3 iota_compare_fusion
  1.1 26.6 %copy.19 = bf16[320,2,4,6,1280]{4,0,3,2,1:T(8,128)(2,1)} copy(bf16[320,2,4,6,1280]{4,2,3,1,0:T(4,128)(2,1)} %param.8) | data formatting | bytes 78643200 | tf_op args[0]
  27.7 47.5 %fusion.5 = bf16[320,8,48]{2,1,0:T(8,128)(2,1)S(1)} fusion(bf16[320,48,1280]{2,0,1:T(8,128)(2,1)} %bitcast.34, bf16[320,8,1280]{2,1,0:T(8,128)(2,1)} %param.9, pred[320,1280]{1,0:T(8,128)(4,1)S(1)} %iota_compare_fusion), kind=kOutput, calls=%fused_computation.10 | convolution fusion | flops 317972480 | bytes 46530560 | tf_op jit(solution)/shard_map/skj,slj->slk/dot_general | solution.py:71
  75.2 1.1 copy.21
  76.4 4.2 %all-to-all-start = ((bf16[320,8,48]{0,2,1:T(8,128)(2,1)}), bf16[320,8,48]{0,2,1:T(8,128)(2,1)S(1)}, u32[]{:S(2)}, u32[]{:S(2)}) async-start(bf16[320,8,48]{0,2,1:T(8,128)(2,1)} %copy.21), calls=%async_computation | async-start | bytes 589824 | tf_op jit(solution)/shard_map/all_to_all | solution.py:74
  80.6 2.6 %fusion.15 = (f32[1280,128]{0,1:T(8,128)S(1)}, f32[1280,128]{0,1:T(8,128)S(1)}) fusion(s32[1280]{0:T(1024)S(1)} %copy-done), kind=kLoop, calls=%fused_computation.18 | loop fusion | flops 1474560 | bytes 1315840 | tf_op jit(solution)/shard_map/cos | solution.py:38
  83.3 0.4 cosine_multiply_fusion
  83.7 3.3 %subtract_convert_fusion = (bf16[1280,9,128]{0,2,1:T(8,128)(2,1)}, bf16[1280,9,128]{0,2,1:T(8,128)(2,1)S(1)}) fusion(f32[1280,128]{0,1:T(8,128)S(1)} %get-tuple-element.27, f32[1280,9]{0,1:T(8,128)S(1)} %get-tuple-element.25, f32[1280,128]{0,1:T(8,128)S(1)} %get-tuple-element.26, f32[1280,9]{0,1:T(8,128)S(1)} %get-tuple-element.24), kind=kLoop, calls=%fused_computation.7 | loop fusion | flops 13271040 | bytes 7301120 | tf_op jit(solution)/shard_map/convert_element_type | solution.py:48
  87.0 0.2 copy.30
  87.2 0.3 reshape.215
  87.5 2.8 %fusion.17 = f32[96,1152]{1,0:T(8,128)S(1)} fusion(bf16[1280,1152]{0,1:T(8,128)(2,1)} %bitcast.36, bf16[48,1280]{1,0:T(8,128)(2,1)S(1)} %get-tuple-element.28, bf16[48,1280]{1,0:T(8,128)(2,1)S(1)} %bitcast.41), kind=kOutput, calls=%fused_computation.25 | convolution fusion | flops 283607040 | bytes 3637248 | tf_op jit(solution)/shard_map/dot_general | solution.py:87
  90.4 1.0 fusion.21
  91.5 0.3 slice_subtract_fusion
  92.0 0.2 fusion.34
  92.2 0.1 multiply_reduce_fusion
  92.3 0.8 reverse.1
  93.2 0.1 multiply_reduce_fusion.1
  93.3 0.1 multiply_reduce_fusion.2
  93.4 0.8 reverse
  94.3 0.1 multiply_reduce_fusion.3
  94.4 0.2 concatenate.11
  94.6 0.2 reshape.220
  94.8 0.7 copy.23
  95.5 5.5 %all-to-all-start.1 = ((f32[4,2,4,1080]{3,2,1,0:T(4,128)}), f32[4,2,4,1080]{3,2,1,0:T(4,128)S(1)}, u32[]{:S(2)}, u32[]{:S(2)}) async-start(f32[4,2,4,1080]{3,2,1,0:T(4,128)} %copy.23), calls=%async_computation.1 | async-start | bytes 294912 | tf_op jit(solution)/shard_map/all_to_all | solution.py:106
  101.0 6.6 %all-to-all-done.1 = f32[4,2,4,1080]{3,2,1,0:T(4,128)S(1)} async-done(((f32[4,2,4,1080]{3,2,1,0:T(4,128)}), f32[4,2,4,1080]{3,2,1,0:T(4,128)S(1)}, u32[]{:S(2)}, u32[]{:S(2)}) %all-to-all-start.1) | async-done | bytes 138272 | tf_op jit(solution)/shard_map/all_to_all | solution.py:106
  107.7 0.7 broadcast_in_dim.30
  108.5 4.0 %all-to-all-start.2 = ((f32[8,2,4,1080]{3,2,1,0:T(4,128)}), f32[8,2,4,1080]{3,2,1,0:T(4,128)S(1)}, u32[]{:S(2)}, u32[]{:S(2)}) async-start(f32[8,2,4,1080]{3,2,1,0:T(4,128)} %broadcast_in_dim.30), calls=%async_computation.2 | async-start | bytes 589824 | tf_op jit(solution)/shard_map/all_to_all | solution.py:109
  112.6 6.6 %all-to-all-done.2 = f32[8,2,4,1080]{3,2,1,0:T(4,128)S(1)} async-done(((f32[8,2,4,1080]{3,2,1,0:T(4,128)}), f32[8,2,4,1080]{3,2,1,0:T(4,128)S(1)}, u32[]{:S(2)}, u32[]{:S(2)}) %all-to-all-start.2) | async-done | bytes 276512 | tf_op jit(solution)/shard_map/all_to_all | solution.py:109
  119.3 0.6 gather_fusion
  119.9 0.6 gather_fusion.1
  120.4 0.7 fusion.50
  (27 shorter events, 0.7 us)
Async XLA Ops:
  27.7 52.9 %copy-start = (s32[1280]{0:T(1024)S(1)}, s32[1280]{0:T(1024)}, u32[]{:S(2)}) copy-start(s32[1280]{0:T(1024)} %param.10) | copy-start | bytes 15364
  76.4 10.7 %all-to-all-start = ((bf16[320,8,48]{0,2,1:T(8,128)(2,1)}), bf16[320,8,48]{0,2,1:T(8,128)(2,1)S(1)}, u32[]{:S(2)}, u32[]{:S(2)}) async-start(bf16[320,8,48]{0,2,1:T(8,128)(2,1)} %copy.21), calls=%async_computation | async-start | bytes 589824 | tf_op jit(solution)/shard_map/all_to_all | solution.py:74
  90.4 1.6 %copy-start.1 = (f32[6]{0:T(128)S(1)}, f32[6]{0:T(128)}, u32[]{:S(2)}) copy-start(f32[6]{0:T(128)} %param.11) | copy-start | bytes 76
  91.4 21.0 %copy-start.2 = (f32[16]{0:T(128)S(1)}, f32[16]{0:T(128)}, u32[]{:S(2)}) copy-start(f32[16]{0:T(128)} %param.13) | copy-start | bytes 196
  91.5 21.1 %copy-start.3 = (s32[16]{0:T(128)S(1)}, s32[16]{0:T(128)}, u32[]{:S(2)}) copy-start(s32[16]{0:T(128)} %param.12) | copy-start | bytes 196
  95.5 12.2 %all-to-all-start.1 = ((f32[4,2,4,1080]{3,2,1,0:T(4,128)}), f32[4,2,4,1080]{3,2,1,0:T(4,128)S(1)}, u32[]{:S(2)}, u32[]{:S(2)}) async-start(f32[4,2,4,1080]{3,2,1,0:T(4,128)} %copy.23), calls=%async_computation.1 | async-start | bytes 294912 | tf_op jit(solution)/shard_map/all_to_all | solution.py:106
  108.5 10.8 %all-to-all-start.2 = ((f32[8,2,4,1080]{3,2,1,0:T(4,128)}), f32[8,2,4,1080]{3,2,1,0:T(4,128)S(1)}, u32[]{:S(2)}, u32[]{:S(2)}) async-start(f32[8,2,4,1080]{3,2,1,0:T(4,128)} %broadcast_in_dim.30), calls=%async_computation.2 | async-start | bytes 589824 | tf_op jit(solution)/shard_map/all_to_all | solution.py:109
where the time goes:
time: 122 us; the launch traced here: 121 us
  matrix products  51.4 us (42%)
  local copies, waits for them, and re-layouts  33.2 us (27%)
  starting transfers between devices  13.8 us (11%)
  waiting for transfers between devices  13.3 us (11%)
  other arithmetic  9.35 us (8%)
    dot_general x1, matrix products, local(): jnp.einsum('skj,slj->slk', coefficient, table_rows, preferred_element_typ...  47.5 us
    unnamed x13, local copies, waits for them, and re-layouts  28.4 us
    all_to_all x1, waiting for transfers between devices, local(): lax.all_to_all(by_strip, 'lev', split_axis=0, concat_axis=0, tiled=True)  6.64 us
    all_to_all x1, waiting for transfers between devices, local(): lax.all_to_all(copies, ('wave', 'cpl'), split_axis=0, concat_axis=0, tile...  6.63 us
    all_to_all x1, starting transfers between devices, local(): lax.all_to_all(by_strip, 'lev', split_axis=0, concat_axis=0, tiled=True)  5.55 us
    all_to_all x1, starting transfers between devices, local(): lax.all_to_all(spec_grid, 'wave', split_axis=1, concat_axis=0, tiled=True)  4.24 us
    all_to_all x1, starting transfers between devices, local(): lax.all_to_all(copies, ('wave', 'cpl'), split_axis=0, concat_axis=0, tile...  3.98 us
    convert_element_type x1, other arithmetic, quarter_tables(): cos_tab.astype(jnp.bfloat16).reshape(slots, width)  3.34 us
  transfers between devices with their start and end apart: 3, of which 2 were waited for; matrix products, arithmetic and copies ran while one was open for 5% of the time, Pallas kernels for 0%

commit v1 on v0

--- a/solution.py
+++ b/solution.py
@@ -71,7 +71,12 @@
     spec_grid = jnp.einsum(
         "skj,slj->slk", coefficient, table_rows, preferred_element_type=jnp.float32
     ).astype(jnp.bfloat16)
-    by_latitude = lax.all_to_all(spec_grid, "wave", split_axis=1, concat_axis=0, tiled=True)
+    by_latitude = jnp.concatenate(
+        lax.all_to_all(
+            jnp.stack(jnp.split(spec_grid, lax.axis_size("wave"), axis=1)), "wave", 0, 0
+        ),
+        axis=0,
+    )
     total_slots = by_latitude.shape[0]
     lat_dev = by_latitude.shape[1]
     rows = lat_dev * fields * levels

time: 122 us -> 122 us (level)
    another operation x0 -> x6, local copies, waits for them, and re-layouts: none -> 1.27 us  [the longest x5 1.01 us: local(): jnp.stack(jnp.split(spec_grid, lax.axis_size('wave'), axis=1))]
where the time goes in v1:
time: 122 us
  matrix products  51.3 us (42%)
  local copies, waits for them, and re-layouts  33.1 us (27%)
  starting transfers between devices  13.8 us (11%)
  waiting for transfers between devices  13.3 us (11%)
  other arithmetic  10.2 us (8%)
    dot_general x1, matrix products, local(): jnp.einsum('skj,slj->slk', coefficient, table_rows, preferred_element_typ...  47.4 us
    unnamed x13, local copies, waits for them, and re-layouts  28.5 us
    all_to_all x1, waiting for transfers between devices, local(): lax.all_to_all(by_strip, 'lev', split_axis=0, concat_axis=0, tiled=True)  6.64 us
    all_to_all x1, waiting for transfers between devices, local(): lax.all_to_all(copies, ('wave', 'cpl'), split_axis=0, concat_axis=0, tile...  6.63 us
    all_to_all x1, starting transfers between devices, local(): lax.all_to_all(by_strip, 'lev', split_axis=0, concat_axis=0, tiled=True)  5.55 us
    all_to_all x1, starting transfers between devices, local(): lax.all_to_all(jnp.stack(jnp.split(spec_grid, lax.axis_size('wave'), axis...  4.24 us
    all_to_all x1, starting transfers between devices, local(): lax.all_to_all(copies, ('wave', 'cpl'), split_axis=0, concat_axis=0, tile...  3.98 us
    convert_element_type x1, other arithmetic, quarter_tables(): cos_tab.astype(jnp.bfloat16).reshape(slots, width)  3.34 us
  transfers between devices with their start and end apart: 3, of which 2 were waited for; matrix products, arithmetic and copies ran while one was open for 5% of the time, Pallas kernels for 0%

profile of v1, /device:TPU:0, one launch (start us, length us, event | category | flops | bytes accessed | tf_op | source)
XLA Modules:
  0.0 121.8 jit_solution(18119571799722693849)
XLA Ops:
  0.0 0.8 dynamic-slice_subtract_fusion
  0.8 0.3 iota_compare_fusion
  1.1 26.6 %copy.22 = bf16[320,2,4,6,1280]{4,0,3,2,1:T(8,128)(2,1)} copy(bf16[320,2,4,6,1280]{4,2,3,1,0:T(4,128)(2,1)} %param.8) | data formatting | bytes 78643200 | tf_op args[0]
  27.7 47.4 %fusion.5 = bf16[320,8,48]{2,1,0:T(8,128)(2,1)S(1)} fusion(bf16[320,48,1280]{2,0,1:T(8,128)(2,1)} %bitcast.38, bf16[320,8,1280]{2,1,0:T(8,128)(2,1)} %param.9, pred[320,1280]{1,0:T(8,128)(4,1)S(1)} %iota_compare_fusion), kind=kOutput, calls=%fused_computation.10 | convolution fusion | flops 317972480 | bytes 46530560 | tf_op jit(solution)/shard_map/skj,slj->slk/dot_general | solution.py:71
  75.2 0.5 slice_bitcast_fusion.3
  75.6 0.1 copy.24
  75.8 0.1 copy.25
  76.1 0.1 copy.27
  76.2 0.8 pad_maximum_fusion
  77.0 4.2 %all-to-all-start = ((bf16[4,320,2,48]{1,3,2,0:T(8,128)(2,1)}), bf16[4,320,2,48]{1,3,2,0:T(8,128)(2,1)S(1)}, u32[]{:S(2)}, u32[]{:S(2)}) async-start(bf16[4,320,2,48]{1,3,2,0:T(8,128)(2,1)} %pad_maximum_fusion), calls=%async_computation | async-start | bytes 589824 | tf_op jit(solution)/shard_map/all_to_all | solution.py:75
  81.3 2.6 %fusion.15 = (f32[1280,128]{0,1:T(8,128)S(1)}, f32[1280,128]{0,1:T(8,128)S(1)}) fusion(s32[1280]{0:T(1024)S(1)} %copy-done), kind=kLoop, calls=%fused_computation.18 | loop fusion | flops 1474560 | bytes 1315840 | tf_op jit(solution)/shard_map/cos | solution.py:38
  83.9 0.4 cosine_multiply_fusion
  84.3 3.3 %subtract_convert_fusion = (bf16[1280,9,128]{0,2,1:T(8,128)(2,1)}, bf16[1280,9,128]{0,2,1:T(8,128)(2,1)S(1)}) fusion(f32[1280,128]{0,1:T(8,128)S(1)} %get-tuple-element.31, f32[1280,9]{0,1:T(8,128)S(1)} %get-tuple-element.29, f32[1280,128]{0,1:T(8,128)S(1)} %get-tuple-element.30, f32[1280,9]{0,1:T(8,128)S(1)} %get-tuple-element.28), kind=kLoop, calls=%fused_computation.7 | loop fusion | flops 13271040 | bytes 7301120 | tf_op jit(solution)/shard_map/convert_element_type | solution.py:48
  87.7 0.2 copy.28
  87.8 0.3 reshape_reshape.6
  88.2 2.8 %fusion.17 = f32[96,1152]{1,0:T(8,128)S(1)} fusion(bf16[1280,1152]{0,1:T(8,128)(2,1)} %bitcast.40, bf16[48,1280]{1,0:T(8,128)(2,1)S(1)} %get-tuple-element.32, bf16[48,1280]{1,0:T(8,128)(2,1)S(1)} %bitcast.43), kind=kOutput, calls=%fused_computation.25 | convolution fusion | flops 283607040 | bytes 3637248 | tf_op jit(solution)/shard_map/dot_general | solution.py:92
  91.1 1.0 fusion.21
  92.1 0.3 slice_subtract_fusion
  92.6 0.2 fusion.34
  92.9 0.8 reverse.1
  94.1 0.8 reverse
  95.1 0.2 concatenate.11
  95.3 0.2 reshape.215
  95.4 0.7 copy.29
  96.1 5.6 %all-to-all-start.1 = ((f32[4,2,4,1080]{3,2,1,0:T(4,128)}), f32[4,2,4,1080]{3,2,1,0:T(4,128)S(1)}, u32[]{:S(2)}, u32[]{:S(2)}) async-start(f32[4,2,4,1080]{3,2,1,0:T(4,128)} %copy.29), calls=%async_computation.1 | async-start | bytes 294912 | tf_op jit(solution)/shard_map/all_to_all | solution.py:111
  101.7 6.6 %all-to-all-done.1 = f32[4,2,4,1080]{3,2,1,0:T(4,128)S(1)} async-done(((f32[4,2,4,1080]{3,2,1,0:T(4,128)}), f32[4,2,4,1080]{3,2,1,0:T(4,128)S(1)}, u32[]{:S(2)}, u32[]{:S(2)}) %all-to-all-start.1) | async-done | bytes 138272 | tf_op jit(solution)/shard_map/all_to_all | solution.py:111
  108.4 0.8 broadcast_in_dim.30
  109.1 4.0 %all-to-all-start.2 = ((f32[8,2,4,1080]{3,2,1,0:T(4,128)}), f32[8,2,4,1080]{3,2,1,0:T(4,128)S(1)}, u32[]{:S(2)}, u32[]{:S(2)}) async-start(f32[8,2,4,1080]{3,2,1,0:T(4,128)} %broadcast_in_dim.30), calls=%async_computation.2 | async-start | bytes 589824 | tf_op jit(solution)/shard_map/all_to_all | solution.py:114
  113.3 6.6 %all-to-all-done.2 = f32[8,2,4,1080]{3,2,1,0:T(4,128)S(1)} async-done(((f32[8,2,4,1080]{3,2,1,0:T(4,128)}), f32[8,2,4,1080]{3,2,1,0:T(4,128)S(1)}, u32[]{:S(2)}, u32[]{:S(2)}) %all-to-all-start.2) | async-done | bytes 276512 | tf_op jit(solution)/shard_map/all_to_all | solution.py:114
  119.9 0.6 gather_fusion
  120.5 0.6 gather_fusion.1
  121.1 0.7 fusion.50
  (32 shorter events, 1.3 us)
Async XLA Ops:
  27.7 53.5 %copy-start = (s32[1280]{0:T(1024)S(1)}, s32[1280]{0:T(1024)}, u32[]{:S(2)}) copy-start(s32[1280]{0:T(1024)} %param.10) | copy-start | bytes 15364
  77.0 10.7 %all-to-all-start = ((bf16[4,320,2,48]{1,3,2,0:T(8,128)(2,1)}), bf16[4,320,2,48]{1,3,2,0:T(8,128)(2,1)S(1)}, u32[]{:S(2)}, u32[]{:S(2)}) async-start(bf16[4,320,2,48]{1,3,2,0:T(8,128)(2,1)} %pad_maximum_fusion), calls=%async_computation | async-start | bytes 589824 | tf_op jit(solution)/shard_map/all_to_all | solution.py:75
  91.0 1.6 %copy-start.1 = (f32[6]{0:T(128)S(1)}, f32[6]{0:T(128)}, u32[]{:S(2)}) copy-start(f32[6]{0:T(128)} %param.11) | copy-start | bytes 76
  92.1 21.0 %copy-start.2 = (f32[16]{0:T(128)S(1)}, f32[16]{0:T(128)}, u32[]{:S(2)}) copy-start(f32[16]{0:T(128)} %param.13) | copy-start | bytes 196
  92.1 21.1 %copy-start.3 = (s32[16]{0:T(128)S(1)}, s32[16]{0:T(128)}, u32[]{:S(2)}) copy-start(s32[16]{0:T(128)} %param.12) | copy-start | bytes 196
  96.1 12.2 %all-to-all-start.1 = ((f32[4,2,4,1080]{3,2,1,0:T(4,128)}), f32[4,2,4,1080]{3,2,1,0:T(4,128)S(1)}, u32[]{:S(2)}, u32[]{:S(2)}) async-start(f32[4,2,4,1080]{3,2,1,0:T(4,128)} %copy.29), calls=%async_computation.1 | async-start | bytes 294912 | tf_op jit(solution)/shard_map/all_to_all | solution.py:111
  109.1 10.8 %all-to-all-start.2 = ((f32[8,2,4,1080]{3,2,1,0:T(4,128)}), f32[8,2,4,1080]{3,2,1,0:T(4,128)S(1)}, u32[]{:S(2)}, u32[]{:S(2)}) async-start(f32[8,2,4,1080]{3,2,1,0:T(4,128)} %broadcast_in_dim.30), calls=%async_computation.2 | async-start | bytes 589824 | tf_op jit(solution)/shard_map/all_to_all | solution.py:114
